TPU v7x, 32 devices: a whole 2x2x4 slice. The times are simulated.
32 devices in a mesh: section: 4 (over y, x), expert: 8 (over z, core).
Axes of the slice: x: 2, y: 2, z: 4, core: 2. Of those that a mesh axis runs over, the one named last changes fastest.
Arguments:
- tokens: bfloat16 [4, 128, 2048], P(None, 'expert'), may hold values from -6 to 6
- norm_gain: float32 [4, 2048], P('section'), may hold values from 0.1 to 1.9
- gate_weight: bfloat16 [4, 16, 2048, 768], P('section', 'expert'), may hold values from -0.125 to 0.125
- up_weight: bfloat16 [4, 16, 2048, 768], P('section', 'expert'), may hold values from -0.125 to 0.125
- down_weight: bfloat16 [4, 16, 768, 2048], P('section', 'expert'), may hold values from -0.21875 to 0.21875
- routes: int32 [4, 4, 128, 8], P('section', None, 'expert'), may hold values from 0 to 15, all different within a row; in each aligned block of 16 rows (0 to 15, 16 to 31, ..., all dimensions but the last counted through in order) at most 12 rows name the same one
- gates: float32 [4, 4, 128, 8], P('section', None, 'expert'), may hold values from 0.1 to 1
Outputs:
- hidden_states: bfloat16 [4, 4, 128, 2048], P('section', None, 'expert')
Inputs may be any that keep to these rules, and one draw needn't show every extreme that they name: `routes`: within one section and micro-batch, the 16 tokens of one device name any one expert at most 12 times, a bound that some expert reaches in some of these blocks; the 8 experts of a token differ.
All inputs are finite; a program needn't handle non-finite values.
Results may differ from a plain program's by a relative error of at most 0.012.
Values may be sent and summed in bfloat16 or wider, within the bound.
No kernel may reach another device: no remote copies, remote signals or barrier semaphores. Data moves between devices by JAX's collectives and lax.ppermute only.
A program may use at most 128 MiB of HBM per device.

v0:
```python
import jax
import jax.numpy as jnp
from jax import lax
from jax.sharding import PartitionSpec as P

MB = 4
EPSILON = 1e-06


def shifted(array, axis, by):
    count = lax.axis_size(axis)
    pairs = [(i, i + by) for i in range(count) if 0 <= i + by < count]
    return lax.ppermute(array, axis, pairs)


def rms_normed(hidden, gain):
    values = hidden.astype(jnp.float32)
    scale = lax.rsqrt(jnp.mean(values * values, axis=-1, keepdims=True) + EPSILON)
    return (values, (values * scale * gain).astype(jnp.bfloat16))


def route_weights(routes, gates, first_expert, local_experts):
    weights = gates / jnp.sum(gates, axis=-1, keepdims=True)
    mine = first_expert + jnp.arange(local_experts, dtype=jnp.int32)
    hit = routes[..., None] == mine
    return jnp.sum(jnp.where(hit, weights[..., None], 0.0), axis=-2)


def on_device(tokens, norm_gain, gate_weight, up_weight, down_weight, routes, gates):
    sections = lax.axis_size("section")
    section_index = lax.axis_index("section")
    expert_index = lax.axis_index("expert")
    local_experts = gate_weight.shape[1]
    gain = norm_gain[0]
    w_gate = gate_weight[0]
    w_up = up_weight[0]
    w_down = down_weight[0]
    all_routes = lax.all_gather(routes[0], "expert", axis=1, tiled=True)
    all_gates = lax.all_gather(gates[0], "expert", axis=1, tiled=True)
    mixing = route_weights(all_routes, all_gates, expert_index * local_experts, local_experts)
    tok_rows = tokens.shape[1]
    width = tokens.shape[2]
    held = jnp.zeros((tok_rows, width), jnp.bfloat16)
    collected = jnp.zeros((MB, tok_rows, width), jnp.bfloat16)
    for moment in range(MB + sections - 1):
        if moment > 0:
            arrived = shifted(held, "section", 1)
        else:
            arrived = held
        batch_index = moment - section_index
        active = (batch_index >= 0) & (batch_index < MB)
        clipped = jnp.clip(batch_index, 0, MB - 1)
        first_rows = lax.dynamic_index_in_dim(tokens, clipped, 0, keepdims=False)
        incoming = jnp.where(section_index == 0, first_rows, arrived)
        weight = lax.dynamic_index_in_dim(mixing, clipped, 0, keepdims=False)
        values, normed = rms_normed(incoming, gain)
        rows = lax.all_gather(normed, "expert", axis=0, tiled=True)
        gate_part = jnp.einsum("td,edf->etf", rows, w_gate, preferred_element_type=jnp.float32)
        up_part = jnp.einsum("td,edf->etf", rows, w_up, preferred_element_type=jnp.float32)
        inner = (jax.nn.silu(gate_part) * up_part).astype(jnp.bfloat16)
        expert_out = jnp.einsum(
            "etf,efd->etd", inner, w_down, preferred_element_type=jnp.float32
        ).astype(jnp.bfloat16)
        partial = jnp.sum(weight.T[:, :, None] * expert_out.astype(jnp.float32), axis=0)
        mixed = lax.psum_scatter(partial, "expert", scatter_dimension=0, tiled=True)
        produced = (values + mixed).astype(jnp.bfloat16)
        held = jnp.where(active, produced, incoming)
        updated = lax.dynamic_update_index_in_dim(collected, held, clipped, 0)
        collected = jnp.where(active, updated, collected)
    return collected[None]


def solution(mesh):
    placed = (
        P(None, "expert", None),
        P("section", None),
        P("section", "expert", None, None),
        P("section", "expert", None, None),
        P("section", "expert", None, None),
        P("section", None, "expert", None),
        P("section", None, "expert", None),
    )
    return jax.shard_map(
        on_device,
        mesh=mesh,
        in_specs=placed,
        out_specs=P("section", None, "expert", None),
        check_vma=False,
    )
```

profile of v0, /device:TPU:0, one launch (start us, length us, event | category | flops | bytes accessed | tf_op | source)
XLA Modules:
  0.0 498.8 jit_solution(13108458287692976375)
XLA Ops:
  7.3 15.9 %all-gather.1 = f32[1,4,128,8]{3,1,0,2:T(4,128)S(1)} all-gather(f32[1,4,16,8]{3,1,0,2:T(4,128)S(1)} %copy.16), channel_id=3, replica_groups=mesh['section'=4,'expert'=8] {'expert'}, dimensions={2}, use_global_device_ids=true | all-gather | bytes 18432 | tf_op jit(solution)/shard_map/all_gather | solution.py:39
  24.5 14.2 %all-gather = s32[1,4,128,8]{3,1,0,2:T(4,128)S(1)} all-gather(s32[1,4,16,8]{3,1,0,2:T(4,128)S(1)} %copy.14), channel_id=2, replica_groups=mesh['section'=4,'expert'=8] {'expert'}, dimensions={2}, use_global_device_ids=true | all-gather | bytes 18432 | tf_op jit(solution)/shard_map/all_gather | solution.py:38
  38.8 1.0 fusion.287
  39.8 0.9 fusion.289
  40.8 14.8 %all_gather.29 = bf16[128,2048]{1,0:T(8,128)(2,1)S(1)} all-gather(bf16[16,2048]{1,0:T(8,128)(2,1)S(1)} %fusion.289), channel_id=1, replica_groups=mesh['section'=4,'expert'=8] {'expert'}, dimensions={0}, use_global_device_ids=true | all-gather | bytes 589824 | tf_op jit(solution)/shard_map/all_gather | solution.py:57
  55.6 3.8 fusion.126
  59.5 7.8 %fusion.123 = f32[128,2048]{1,0:T(8,128)} fusion(bf16[1,2,768,2048]{3,2,1,0:T(8,128)(2,1)} %param.11, f32[2,128]{1,0:T(2,128)S(1)} %get-tuple-element.35, bf16[1,2,2048,768]{3,2,1,0:T(8,128)(2,1)} %param.10, f32[2,128,768]{2,1,0:T(8,128)S(1)} %fusion.126, bf16[128,2048]{1,0:T(8,128)(2,1)S(1)} %all_gather.29), kind=kOutput, calls=%fused_computation.69 | convolution fusion | flops 1613627392 | bytes 14943232 | tf_op jit(solution)/shard_map/etf,efd->etd/dot_general | solution.py:61
  67.4 33.9 %reduce-scatter.8.cloned.1.call-done = f32[16,2048]{1,0:T(8,128)} async-done(((f32[128,2048]{1,0:T(8,128)}), f32[16,2048]{1,0:T(8,128)}) %reduce-scatter.8.cloned.1.call-update) | async-done | bytes 131088 | tf_op jit(solution)/shard_map/reduce_scatter | solution.py:65
  101.3 0.9 bitcast_dynamic-update-slice_fusion
  102.2 3.4 collective-permute-start
  105.7 1.9 collective-permute-done
  107.8 15.0 %all_gather.30 = bf16[128,2048]{1,0:T(8,128)(2,1)S(1)} all-gather(bf16[16,2048]{1,0:T(8,128)(2,1)S(1)} %fusion.293), channel_id=1, replica_groups=mesh['section'=4,'expert'=8] {'expert'}, dimensions={0}, use_global_device_ids=true | all-gather | bytes 589824 | tf_op jit(solution)/shard_map/all_gather | solution.py:57
  122.8 3.8 fusion.129
  126.6 7.8 %fusion.120 = f32[128,2048]{1,0:T(8,128)} fusion(bf16[1,2,768,2048]{3,2,1,0:T(8,128)(2,1)} %param.11, f32[2,128]{1,0:T(2,128)S(1)} %get-tuple-element.34, bf16[1,2,2048,768]{3,2,1,0:T(8,128)(2,1)} %param.10, f32[2,128,768]{2,1,0:T(8,128)S(1)} %fusion.129, bf16[128,2048]{1,0:T(8,128)(2,1)S(1)} %all_gather.30), kind=kOutput, calls=%fused_computation.68 | convolution fusion | flops 1613627392 | bytes 14943232 | tf_op jit(solution)/shard_map/etf,efd->etd/dot_general | solution.py:61
  134.4 31.6 %reduce-scatter.10.cloned.1.call-done = f32[16,2048]{1,0:T(8,128)} async-done(((f32[128,2048]{1,0:T(8,128)}), f32[16,2048]{1,0:T(8,128)}) %reduce-scatter.10.cloned.1.call-update) | async-done | bytes 131088 | tf_op jit(solution)/shard_map/reduce_scatter | solution.py:65
  167.0 3.2 collective-permute-start.1
  170.2 1.9 collective-permute-done.1
  172.3 15.2 %all_gather.31 = bf16[128,2048]{1,0:T(8,128)(2,1)S(1)} all-gather(bf16[16,2048]{1,0:T(8,128)(2,1)S(1)} %fusion.297), channel_id=1, replica_groups=mesh['section'=4,'expert'=8] {'expert'}, dimensions={0}, use_global_device_ids=true | all-gather | bytes 589824 | tf_op jit(solution)/shard_map/all_gather | solution.py:57
  187.5 3.8 fusion.132
  191.3 7.8 %fusion.117 = f32[128,2048]{1,0:T(8,128)} fusion(bf16[1,2,768,2048]{3,2,1,0:T(8,128)(2,1)} %param.11, f32[2,128]{1,0:T(2,128)S(1)} %get-tuple-element.33, bf16[1,2,2048,768]{3,2,1,0:T(8,128)(2,1)} %param.10, f32[2,128,768]{2,1,0:T(8,128)S(1)} %fusion.132, bf16[128,2048]{1,0:T(8,128)(2,1)S(1)} %all_gather.31), kind=kOutput, calls=%fused_computation.67 | convolution fusion | flops 1613627392 | bytes 14943232 | tf_op jit(solution)/shard_map/etf,efd->etd/dot_general | solution.py:61
  199.2 31.7 %reduce-scatter.12.cloned.1.call-done = f32[16,2048]{1,0:T(8,128)} async-done(((f32[128,2048]{1,0:T(8,128)}), f32[16,2048]{1,0:T(8,128)}) %reduce-scatter.12.cloned.1.call-update) | async-done | bytes 131088 | tf_op jit(solution)/shard_map/reduce_scatter | solution.py:65
  230.9 0.9 fusion.329
  231.9 3.6 collective-permute-start.2
  235.5 1.9 collective-permute-done.2
  237.6 15.0 %all_gather.32 = bf16[128,2048]{1,0:T(8,128)(2,1)S(1)} all-gather(bf16[16,2048]{1,0:T(8,128)(2,1)S(1)} %fusion.301), channel_id=1, replica_groups=mesh['section'=4,'expert'=8] {'expert'}, dimensions={0}, use_global_device_ids=true | all-gather | bytes 589824 | tf_op jit(solution)/shard_map/all_gather | solution.py:57
  252.6 3.8 fusion.135
  256.4 7.8 %fusion.114 = f32[128,2048]{1,0:T(8,128)} fusion(bf16[1,2,768,2048]{3,2,1,0:T(8,128)(2,1)} %param.11, f32[2,128]{1,0:T(2,128)S(1)} %get-tuple-element.32, bf16[1,2,2048,768]{3,2,1,0:T(8,128)(2,1)} %param.10, f32[2,128,768]{2,1,0:T(8,128)S(1)} %fusion.135, bf16[128,2048]{1,0:T(8,128)(2,1)S(1)} %all_gather.32), kind=kOutput, calls=%fused_computation.66 | convolution fusion | flops 1613627392 | bytes 14943232 | tf_op jit(solution)/shard_map/etf,efd->etd/dot_general | solution.py:61
  264.3 31.5 %reduce-scatter.14.cloned.1.call-done = f32[16,2048]{1,0:T(8,128)} async-done(((f32[128,2048]{1,0:T(8,128)}), f32[16,2048]{1,0:T(8,128)}) %reduce-scatter.14.cloned.1.call-update) | async-done | bytes 131088 | tf_op jit(solution)/shard_map/reduce_scatter | solution.py:65
  295.8 0.9 fusion.328
  296.7 3.7 collective-permute-start.3
  300.4 1.9 collective-permute-done.3
  302.5 15.0 %all_gather.33 = bf16[128,2048]{1,0:T(8,128)(2,1)S(1)} all-gather(bf16[16,2048]{1,0:T(8,128)(2,1)S(1)} %fusion.305), channel_id=1, replica_groups=mesh['section'=4,'expert'=8] {'expert'}, dimensions={0}, use_global_device_ids=true | all-gather | bytes 589824 | tf_op jit(solution)/shard_map/all_gather | solution.py:57
  317.6 3.8 fusion.138
  321.4 7.8 %fusion.111 = f32[128,2048]{1,0:T(8,128)} fusion(bf16[1,2,768,2048]{3,2,1,0:T(8,128)(2,1)} %param.11, f32[2,128]{1,0:T(2,128)S(1)} %get-tuple-element.31, bf16[1,2,2048,768]{3,2,1,0:T(8,128)(2,1)} %param.10, f32[2,128,768]{2,1,0:T(8,128)S(1)} %fusion.138, bf16[128,2048]{1,0:T(8,128)(2,1)S(1)} %all_gather.33), kind=kOutput, calls=%fused_computation.65 | convolution fusion | flops 1613627392 | bytes 14943232 | tf_op jit(solution)/shard_map/etf,efd->etd/dot_general | solution.py:61
  329.2 31.7 %reduce-scatter.16.cloned.1.call-done = f32[16,2048]{1,0:T(8,128)} async-done(((f32[128,2048]{1,0:T(8,128)}), f32[16,2048]{1,0:T(8,128)}) %reduce-scatter.16.cloned.1.call-update) | async-done | bytes 131088 | tf_op jit(solution)/shard_map/reduce_scatter | solution.py:65
  361.8 3.3 collective-permute-start.4
  365.2 1.9 collective-permute-done.4
  367.3 15.2 %all_gather.34 = bf16[128,2048]{1,0:T(8,128)(2,1)S(1)} all-gather(bf16[16,2048]{1,0:T(8,128)(2,1)S(1)} %fusion.309), channel_id=1, replica_groups=mesh['section'=4,'expert'=8] {'expert'}, dimensions={0}, use_global_device_ids=true | all-gather | bytes 589824 | tf_op jit(solution)/shard_map/all_gather | solution.py:57
  382.5 3.8 fusion.141
  386.3 7.8 %fusion.108 = f32[128,2048]{1,0:T(8,128)} fusion(bf16[1,2,768,2048]{3,2,1,0:T(8,128)(2,1)} %param.11, f32[2,128]{1,0:T(2,128)S(1)} %get-tuple-element.30, bf16[1,2,2048,768]{3,2,1,0:T(8,128)(2,1)} %param.10, f32[2,128,768]{2,1,0:T(8,128)S(1)} %fusion.141, bf16[128,2048]{1,0:T(8,128)(2,1)S(1)} %all_gather.34), kind=kOutput, calls=%fused_computation.64 | convolution fusion | flops 1613627392 | bytes 14943232 | tf_op jit(solution)/shard_map/etf,efd->etd/dot_general | solution.py:61
  394.1 31.5 %reduce-scatter.18.cloned.1.call-done = f32[16,2048]{1,0:T(8,128)} async-done(((f32[128,2048]{1,0:T(8,128)}), f32[16,2048]{1,0:T(8,128)}) %reduce-scatter.18.cloned.1.call-update) | async-done | bytes 131088 | tf_op jit(solution)/shard_map/reduce_scatter | solution.py:65
  426.5 3.7 collective-permute-start.5
  430.2 1.9 collective-permute-done.5
  432.3 15.0 %all_gather.35 = bf16[128,2048]{1,0:T(8,128)(2,1)S(1)} all-gather(bf16[16,2048]{1,0:T(8,128)(2,1)S(1)} %fusion.313), channel_id=1, replica_groups=mesh['section'=4,'expert'=8] {'expert'}, dimensions={0}, use_global_device_ids=true | all-gather | bytes 589824 | tf_op jit(solution)/shard_map/all_gather | solution.py:57
  447.4 3.8 fusion.144
  451.1 7.8 %fusion.105 = f32[128,2048]{1,0:T(8,128)} fusion(bf16[1,2,768,2048]{3,2,1,0:T(8,128)(2,1)} %param.11, f32[2,128]{1,0:T(2,128)S(1)} %get-tuple-element.29, bf16[1,2,2048,768]{3,2,1,0:T(8,128)(2,1)} %param.10, f32[2,128,768]{2,1,0:T(8,128)S(1)} %fusion.144, bf16[128,2048]{1,0:T(8,128)(2,1)S(1)} %all_gather.35), kind=kOutput, calls=%fused_computation.63 | convolution fusion | flops 1613627392 | bytes 14943232 | tf_op jit(solution)/shard_map/etf,efd->etd/dot_general | solution.py:61
  459.6 30.7 %reduce-scatter.20.cloned.1.call-done = f32[16,2048]{1,0:T(8,128)} async-done(((f32[128,2048]{1,0:T(8,128)}), f32[16,2048]{1,0:T(8,128)}) %reduce-scatter.20.cloned.1.call-update) | async-done | bytes 131088 | tf_op jit(solution)/shard_map/reduce_scatter | solution.py:65
  490.4 1.6 fusion.325
  (51 shorter events, 7.6 us)
Async XLA Ops:
  6.5 94.7 %reduce-scatter.8.cloned.1.call-start = ((), (), s32[]{:S(2)}) async-start(), calls=%async_computation.7 | async-start | bytes 1179648 | tf_op jit(solution)/shard_map/reduce_scatter | solution.py:65
  59.5 41.8 %copy-start = (bf16[4,16,2048]{2,1,0:T(8,128)(2,1)S(1)}, bf16[4,16,2048]{2,1,0:T(8,128)(2,1)}, u32[]{:S(2)}) copy-start(bf16[4,16,2048]{2,1,0:T(8,128)(2,1)} %param.7) | copy-start | bytes 786436
  59.5 48.2 %copy-start.1 = (f32[1,2048]{1,0:T(1,128)S(1)}, f32[1,2048]{1,0:T(1,128)}, u32[]{:S(2)}) copy-start(f32[1,2048]{1,0:T(1,128)} %param.8) | copy-start | bytes 24580
  67.3 98.7 %reduce-scatter.10.cloned.1.call-start = ((), (), s32[]{:S(2)}) async-start(), calls=%async_computation.8 | async-start | bytes 1179648 | tf_op jit(solution)/shard_map/reduce_scatter | solution.py:65
  102.2 5.3 %collective-permute-start = (bf16[16,2048]{1,0:T(8,128)(2,1)S(1)}, bf16[16,2048]{1,0:T(8,128)(2,1)S(1)}, u32[]{:S(2)}, u32[]{:S(2)}) collective-permute-start(bf16[16,2048]{1,0:T(8,128)(2,1)S(1)} %get-tuple-element.28), channel_id=1, source_target_pairs={{0,8},{8,16},{16,24},{1,9},{9,17},{17,25},{2,10},{10,18},{18,26},{... | collective-permute-start | bytes 196616 | tf_op jit(solution)/shard_map/ppermute | solution.py:13
  134.4 96.5 %reduce-scatter.12.cloned.1.call-start = ((), (), s32[]{:S(2)}) async-start(), calls=%async_computation.9 | async-start | bytes 1179648 | tf_op jit(solution)/shard_map/reduce_scatter | solution.py:65
  167.0 5.1 %collective-permute-start.1 = (bf16[16,2048]{1,0:T(8,128)(2,1)S(1)}, bf16[16,2048]{1,0:T(8,128)(2,1)S(1)}, u32[]{:S(2)}, u32[]{:S(2)}) collective-permute-start(bf16[16,2048]{1,0:T(8,128)(2,1)S(1)} %get-tuple-element.24), channel_id=1, source_target_pairs={{0,8},{8,16},{16,24},{1,9},{9,17},{17,25},{2,10},{10,18},{18,26},{... | collective-permute-start | bytes 196616 | tf_op jit(solution)/shard_map/ppermute | solution.py:13
  199.1 96.7 %reduce-scatter.14.cloned.1.call-start = ((), (), s32[]{:S(2)}) async-start(), calls=%async_computation.10 | async-start | bytes 1179648 | tf_op jit(solution)/shard_map/reduce_scatter | solution.py:65
  231.9 5.5 %collective-permute-start.2 = (bf16[16,2048]{1,0:T(8,128)(2,1)S(1)}, bf16[16,2048]{1,0:T(8,128)(2,1)S(1)}, u32[]{:S(2)}, u32[]{:S(2)}) collective-permute-start(bf16[16,2048]{1,0:T(8,128)(2,1)S(1)} %get-tuple-element.20), channel_id=1, source_target_pairs={{0,8},{8,16},{16,24},{1,9},{9,17},{17,25},{2,10},{10,18},{18,26},{... | collective-permute-start | bytes 196616 | tf_op jit(solution)/shard_map/ppermute | solution.py:13
  264.3 96.6 %reduce-scatter.16.cloned.1.call-start = ((), (), s32[]{:S(2)}) async-start(), calls=%async_computation.11 | async-start | bytes 1179648 | tf_op jit(solution)/shard_map/reduce_scatter | solution.py:65
  296.7 5.5 %collective-permute-start.3 = (bf16[16,2048]{1,0:T(8,128)(2,1)S(1)}, bf16[16,2048]{1,0:T(8,128)(2,1)S(1)}, u32[]{:S(2)}, u32[]{:S(2)}) collective-permute-start(bf16[16,2048]{1,0:T(8,128)(2,1)S(1)} %get-tuple-element.16), channel_id=1, source_target_pairs={{0,8},{8,16},{16,24},{1,9},{9,17},{17,25},{2,10},{10,18},{18,26},{... | collective-permute-start | bytes 196616 | tf_op jit(solution)/shard_map/ppermute | solution.py:13
  329.2 96.4 %reduce-scatter.18.cloned.1.call-start = ((), (), s32[]{:S(2)}) async-start(), calls=%async_computation.12 | async-start | bytes 1179648 | tf_op jit(solution)/shard_map/reduce_scatter | solution.py:65
  361.8 5.2 %collective-permute-start.4 = (bf16[16,2048]{1,0:T(8,128)(2,1)S(1)}, bf16[16,2048]{1,0:T(8,128)(2,1)S(1)}, u32[]{:S(2)}, u32[]{:S(2)}) collective-permute-start(bf16[16,2048]{1,0:T(8,128)(2,1)S(1)} %get-tuple-element.12), channel_id=1, source_target_pairs={{0,8},{8,16},{16,24},{1,9},{9,17},{17,25},{2,10},{10,18},{18,26},{... | collective-permute-start | bytes 196616 | tf_op jit(solution)/shard_map/ppermute | solution.py:13
  394.1 96.3 %reduce-scatter.20.cloned.1.call-start = ((), (), s32[]{:S(2)}) async-start(), calls=%async_computation.13 | async-start | bytes 1179648 | tf_op jit(solution)/shard_map/reduce_scatter | solution.py:65
  426.5 5.6 %collective-permute-start.5 = (bf16[16,2048]{1,0:T(8,128)(2,1)S(1)}, bf16[16,2048]{1,0:T(8,128)(2,1)S(1)}, u32[]{:S(2)}, u32[]{:S(2)}) collective-permute-start(bf16[16,2048]{1,0:T(8,128)(2,1)S(1)} %get-tuple-element.8), channel_id=1, source_target_pairs={{0,8},{8,16},{16,24},{1,9},{9,17},{17,25},{2,10},{10,18},{18,26},{... | collective-permute-start | bytes 196616 | tf_op jit(solution)/shard_map/ppermute | solution.py:13
Sparse Core Ops, SparseCore 0:
  67.4 33.7 reduce-scatter.7
  134.5 31.4 reduce-scatter.9
  199.2 31.6 reduce-scatter.11
  264.4 31.3 reduce-scatter.13
  329.3 31.5 reduce-scatter.15
  394.2 31.3 reduce-scatter.17
  459.0 31.2 reduce-scatter.19
where the time goes:
time: 500 us; the launch traced here: 499 us
  waiting for transfers between devices  234 us (47%)
  blocking collectives  135 us (27%)
  matrix products  80.9 us (16%)
  starting transfers between devices  21.1 us (4%)
  between operations  13.8 us (3%)
  other arithmetic  11.1 us (2%)
    reduce_scatter x7, waiting for transfers between devices, on_device(): mixed = lax.psum_scatter(partial, 'expert', scatter_dimension=0, tiled=True)  223 us
    all_gather x7, blocking collectives, on_device(): rows = lax.all_gather(normed, 'expert', axis=0, tiled=True)  105 us
    dot_general x7, matrix products, on_device(): jnp.einsum('etf,efd->etd', inner, w_down, preferred_element_type=jnp.floa...  54.5 us
    dot_general x7, matrix products, on_device(): jnp.einsum('td,edf->etf', rows, w_gate, preferred_element_type=jnp.float32)  26.4 us
    ppermute x6, starting transfers between devices, shifted(): return lax.ppermute(array, axis, pairs)  20.8 us
    all_gather x1, blocking collectives, on_device(): all_gates = lax.all_gather(gates[0], 'expert', axis=1, tiled=True)  15.9 us
    all_gather x1, blocking collectives, on_device(): all_routes = lax.all_gather(routes[0], 'expert', axis=1, tiled=True)  14.2 us
    ppermute x6, waiting for transfers between devices, shifted(): return lax.ppermute(array, axis, pairs)  11.3 us
  transfers between devices with their start and end apart: 13, of which 13 were waited for; matrix products, arithmetic and copies ran while one was open for 0% of the time, Pallas kernels for 0%

commit v1 on v0

--- a/solution.py
+++ b/solution.py
@@ -54,7 +54,14 @@
         incoming = jnp.where(section_index == 0, first_rows, arrived)
         weight = lax.dynamic_index_in_dim(mixing, clipped, 0, keepdims=False)
         values, normed = rms_normed(incoming, gain)
-        rows = lax.all_gather(normed, "expert", axis=0, tiled=True)
+        count_2 = lax.axis_size("expert")
+        forward = [(i_2, (i_2 + 1) % count_2) for i_2 in range(count_2)]
+        parts = [normed]
+        for stride in range(1, count_2):
+            parts = [lax.ppermute(parts[0], "expert", forward), *parts]
+        result = jnp.concatenate(parts, axis=0)
+        offset = (lax.axis_index("expert") + 1) * parts[-1].shape[0]
+        rows = jnp.roll(result, offset, axis=0)
         gate_part = jnp.einsum("td,edf->etf", rows, w_gate, preferred_element_type=jnp.float32)
         up_part = jnp.einsum("td,edf->etf", rows, w_up, preferred_element_type=jnp.float32)
         inner = (jax.nn.silu(gate_part) * up_part).astype(jnp.bfloat16)

time: 500 us -> 653 us (1.31)
  waiting for transfers between devices: 234 us -> 488 us
  blocking collectives: 135 us -> 28.5 us
    ppermute x0 -> x49, waiting for transfers between devices: none -> 258 us  [on_device(): parts = [lax.ppermute(parts[0], 'expert', forward), *parts]]
    all_gather x7 -> x0, blocking collectives: 105 us -> none  [on_device(): rows = lax.all_gather(normed, 'expert', axis=0, tiled=True)]
  transfers between devices with their start and end apart: 13 -> 62, of which waited for: 13 -> 60; matrix products, arithmetic and copies ran while one was open for 0% -> 0% of each run, Pallas kernels for 0% -> 0%
where the time goes in v1:
time: 653 us; the launch traced here: 652 us
  waiting for transfers between devices  488 us (75%)
  matrix products  82.6 us (13%)
  blocking collectives  28.5 us (4%)
  starting transfers between devices  23.8 us (4%)
  between operations  14.2 us (2%)
  other arithmetic  12.5 us (2%)
    ppermute x49, waiting for transfers between devices, on_device(): parts = [lax.ppermute(parts[0], 'expert', forward), *parts]  258 us
    reduce_scatter x7, waiting for transfers between devices, on_device(): mixed = lax.psum_scatter(partial, 'expert', scatter_dimension=0, tiled=True)  219 us
    dot_general x7, matrix products, on_device(): jnp.einsum('etf,efd->etd', inner, w_down, preferred_element_type=jnp.floa...  55.3 us
    dot_general x7, matrix products, on_device(): jnp.einsum('td,edf->etf', rows, w_gate, preferred_element_type=jnp.float32)  27.2 us
    ppermute x6, starting transfers between devices, shifted(): return lax.ppermute(array, axis, pairs)  21.5 us
    all_gather x1, blocking collectives, on_device(): all_gates = lax.all_gather(gates[0], 'expert', axis=1, tiled=True)  14.4 us
    all_gather x1, blocking collectives, on_device(): all_routes = lax.all_gather(routes[0], 'expert', axis=1, tiled=True)  14.2 us
  transfers between devices with their start and end apart: 62, of which 60 were waited for; matrix products, arithmetic and copies ran while one was open for 0% of the time, Pallas kernels for 0%

profile of v1, /device:TPU:0, one launch (start us, length us, event | category | flops | bytes accessed | tf_op | source)
XLA Modules:
  0.0 652.4 jit_solution(10869019666607176222)
XLA Ops:
  9.0 6.0 collective-permute-done
  15.0 5.5 collective-permute-done.1
  21.2 14.4 %all-gather.1 = f32[1,4,128,8]{3,1,0,2:T(4,128)S(1)} all-gather(f32[1,4,16,8]{3,1,0,2:T(4,128)S(1)} %copy.16), channel_id=3, replica_groups=mesh['section'=4,'expert'=8] {'expert'}, dimensions={2}, use_global_device_ids=true | all-gather | bytes 18432 | tf_op jit(solution)/shard_map/all_gather | solution.py:39
  37.4 14.2 %all-gather = s32[1,4,128,8]{3,1,0,2:T(4,128)S(1)} all-gather(s32[1,4,16,8]{3,1,0,2:T(4,128)S(1)} %copy.14), channel_id=2, replica_groups=mesh['section'=4,'expert'=8] {'expert'}, dimensions={2}, use_global_device_ids=true | all-gather | bytes 18432 | tf_op jit(solution)/shard_map/all_gather | solution.py:38
  73.1 7.9 %fusion.123 = f32[128,2048]{1,0:T(8,128)} fusion(bf16[1,2,768,2048]{3,2,1,0:T(8,128)(2,1)} %param.13, f32[2,128]{1,0:T(2,128)S(1)} %get-tuple-element.36, bf16[1,2,2048,768]{3,2,1,0:T(8,128)(2,1)} %param.12, f32[2,128,768]{2,1,0:T(8,128)S(1)} %fusion.126, s32[]{:T(128)S(6)} %select_n.252, bf16[128,2048]{1,0:T(8,128)(2,1)S(1)} %constant_dynamic-update-slice_fusion), kind=kOutput, calls=%fused_computation.69 | convolution fusion | flops 1614675968 | bytes 14943236 | tf_op jit(solution)/shard_map/etf,efd->etd/dot_general | solution.py:68
  81.1 31.0 %reduce-scatter.8.cloned.1.call-done = f32[16,2048]{1,0:T(8,128)} async-done(((f32[128,2048]{1,0:T(8,128)}), f32[16,2048]{1,0:T(8,128)}) %reduce-scatter.8.cloned.1.call-update) | async-done | bytes 131088 | tf_op jit(solution)/shard_map/reduce_scatter | solution.py:72
  124.5 5.5 collective-permute-done.9
  130.0 5.5 collective-permute-done.10
  135.5 5.5 collective-permute-done.11
  141.0 5.5 collective-permute-done.12
  146.5 5.5 collective-permute-done.13
  152.0 5.5 collective-permute-done.14
  161.5 7.9 %fusion.120 = f32[128,2048]{1,0:T(8,128)} fusion(bf16[1,2,768,2048]{3,2,1,0:T(8,128)(2,1)} %param.13, f32[2,128]{1,0:T(2,128)S(1)} %get-tuple-element.35, bf16[1,2,2048,768]{3,2,1,0:T(8,128)(2,1)} %param.12, f32[2,128,768]{2,1,0:T(8,128)S(1)} %fusion.129, s32[]{:T(128)S(6)} %select_n.252, bf16[128,2048]{1,0:T(8,128)(2,1)S(1)} %constant_dynamic-update-slice_fusion.8), kind=kOutput, calls=%fused_computation.68 | convolution fusion | flops 1614675968 | bytes 14943236 | tf_op jit(solution)/shard_map/etf,efd->etd/dot_general | solution.py:68
  169.4 31.3 %reduce-scatter.10.cloned.1.call-done = f32[16,2048]{1,0:T(8,128)} async-done(((f32[128,2048]{1,0:T(8,128)}), f32[16,2048]{1,0:T(8,128)}) %reduce-scatter.10.cloned.1.call-update) | async-done | bytes 131088 | tf_op jit(solution)/shard_map/reduce_scatter | solution.py:72
  213.0 5.5 collective-permute-done.17
  218.5 5.5 collective-permute-done.18
  224.0 5.5 collective-permute-done.19
  229.5 5.5 collective-permute-done.20
  235.0 5.5 collective-permute-done.21
  240.5 5.5 collective-permute-done.22
  250.1 7.9 %fusion.117 = f32[128,2048]{1,0:T(8,128)} fusion(bf16[1,2,768,2048]{3,2,1,0:T(8,128)(2,1)} %param.13, f32[2,128]{1,0:T(2,128)S(1)} %get-tuple-element.34, bf16[1,2,2048,768]{3,2,1,0:T(8,128)(2,1)} %param.12, f32[2,128,768]{2,1,0:T(8,128)S(1)} %fusion.132, s32[]{:T(128)S(6)} %select_n.252, bf16[128,2048]{1,0:T(8,128)(2,1)S(1)} %constant_dynamic-update-slice_fusion.16), kind=kOutput, calls=%fused_computation.67 | convolution fusion | flops 1614675968 | bytes 14943236 | tf_op jit(solution)/shard_map/etf,efd->etd/dot_general | solution.py:68
  258.1 31.5 %reduce-scatter.12.cloned.1.call-done = f32[16,2048]{1,0:T(8,128)} async-done(((f32[128,2048]{1,0:T(8,128)}), f32[16,2048]{1,0:T(8,128)}) %reduce-scatter.12.cloned.1.call-update) | async-done | bytes 131088 | tf_op jit(solution)/shard_map/reduce_scatter | solution.py:72
  301.7 5.5 collective-permute-done.25
  307.2 5.5 collective-permute-done.26
  312.7 5.5 collective-permute-done.27
  318.2 5.5 collective-permute-done.28
  323.7 5.5 collective-permute-done.29
  329.2 5.5 collective-permute-done.30
  338.7 7.9 %fusion.114 = f32[128,2048]{1,0:T(8,128)} fusion(bf16[1,2,768,2048]{3,2,1,0:T(8,128)(2,1)} %param.13, f32[2,128]{1,0:T(2,128)S(1)} %get-tuple-element.33, bf16[1,2,2048,768]{3,2,1,0:T(8,128)(2,1)} %param.12, f32[2,128,768]{2,1,0:T(8,128)S(1)} %fusion.135, s32[]{:T(128)S(6)} %select_n.252, bf16[128,2048]{1,0:T(8,128)(2,1)S(1)} %constant_dynamic-update-slice_fusion.24), kind=kOutput, calls=%fused_computation.66 | convolution fusion | flops 1614675968 | bytes 14943236 | tf_op jit(solution)/shard_map/etf,efd->etd/dot_general | solution.py:68
  346.8 31.2 %reduce-scatter.14.cloned.1.call-done = f32[16,2048]{1,0:T(8,128)} async-done(((f32[128,2048]{1,0:T(8,128)}), f32[16,2048]{1,0:T(8,128)}) %reduce-scatter.14.cloned.1.call-update) | async-done | bytes 131088 | tf_op jit(solution)/shard_map/reduce_scatter | solution.py:72
  390.2 5.5 collective-permute-done.33
  395.7 5.5 collective-permute-done.34
  401.2 5.5 collective-permute-done.35
  406.6 5.5 collective-permute-done.36
  412.1 5.5 collective-permute-done.37
  417.6 5.5 collective-permute-done.38
  427.2 7.9 %fusion.111 = f32[128,2048]{1,0:T(8,128)} fusion(bf16[1,2,768,2048]{3,2,1,0:T(8,128)(2,1)} %param.13, f32[2,128]{1,0:T(2,128)S(1)} %get-tuple-element.32, bf16[1,2,2048,768]{3,2,1,0:T(8,128)(2,1)} %param.12, f32[2,128,768]{2,1,0:T(8,128)S(1)} %fusion.138, s32[]{:T(128)S(6)} %select_n.252, bf16[128,2048]{1,0:T(8,128)(2,1)S(1)} %constant_dynamic-update-slice_fusion.32), kind=kOutput, calls=%fused_computation.65 | convolution fusion | flops 1614675968 | bytes 14943236 | tf_op jit(solution)/shard_map/etf,efd->etd/dot_general | solution.py:68
  435.2 31.5 %reduce-scatter.16.cloned.1.call-done = f32[16,2048]{1,0:T(8,128)} async-done(((f32[128,2048]{1,0:T(8,128)}), f32[16,2048]{1,0:T(8,128)}) %reduce-scatter.16.cloned.1.call-update) | async-done | bytes 131088 | tf_op jit(solution)/shard_map/reduce_scatter | solution.py:72
  479.0 5.5 collective-permute-done.41
  484.5 5.5 collective-permute-done.42
  501.0 5.5 collective-permute-done.45
  516.0 7.9 %fusion.108 = f32[128,2048]{1,0:T(8,128)} fusion(bf16[1,2,768,2048]{3,2,1,0:T(8,128)(2,1)} %param.13, f32[2,128]{1,0:T(2,128)S(1)} %get-tuple-element.31, bf16[1,2,2048,768]{3,2,1,0:T(8,128)(2,1)} %param.12, f32[2,128,768]{2,1,0:T(8,128)S(1)} %fusion.141, s32[]{:T(128)S(6)} %select_n.252, bf16[128,2048]{1,0:T(8,128)(2,1)S(1)} %constant_dynamic-update-slice_fusion.40), kind=kOutput, calls=%fused_computation.64 | convolution fusion | flops 1614675968 | bytes 14943236 | tf_op jit(solution)/shard_map/etf,efd->etd/dot_general | solution.py:68
  524.0 31.3 %reduce-scatter.18.cloned.1.call-done = f32[16,2048]{1,0:T(8,128)} async-done(((f32[128,2048]{1,0:T(8,128)}), f32[16,2048]{1,0:T(8,128)}) %reduce-scatter.18.cloned.1.call-update) | async-done | bytes 131088 | tf_op jit(solution)/shard_map/reduce_scatter | solution.py:72
  578.4 5.5 collective-permute-done.51
  583.9 5.5 collective-permute-done.52
  594.8 5.5 collective-permute-done.54
  604.4 7.9 %fusion.105 = f32[128,2048]{1,0:T(8,128)} fusion(bf16[1,2,768,2048]{3,2,1,0:T(8,128)(2,1)} %param.13, f32[2,128]{1,0:T(2,128)S(1)} %get-tuple-element.30, bf16[1,2,2048,768]{3,2,1,0:T(8,128)(2,1)} %param.12, f32[2,128,768]{2,1,0:T(8,128)S(1)} %fusion.144, s32[]{:T(128)S(6)} %select_n.252, bf16[128,2048]{1,0:T(8,128)(2,1)S(1)} %constant_dynamic-update-slice_fusion.48), kind=kOutput, calls=%fused_computation.63 | convolution fusion | flops 1614675968 | bytes 14943236 | tf_op jit(solution)/shard_map/etf,efd->etd/dot_general | solution.py:68
  613.0 31.0 %reduce-scatter.20.cloned.1.call-done = f32[16,2048]{1,0:T(8,128)} async-done(((f32[128,2048]{1,0:T(8,128)}), f32[16,2048]{1,0:T(8,128)}) %reduce-scatter.20.cloned.1.call-update) | async-done | bytes 131088 | tf_op jit(solution)/shard_map/reduce_scatter | solution.py:72
  (198 shorter events, 159.5 us)
Async XLA Ops:
  6.5 105.6 %reduce-scatter.8.cloned.1.call-start = ((), (), s32[]{:S(2)}) async-start(), calls=%async_computation.7 | async-start | bytes 1179648 | tf_op jit(solution)/shard_map/reduce_scatter | solution.py:72
  8.5 6.5 collective-permute-start
  15.0 5.5 collective-permute-start.1
  20.4 15.4 %collective-permute-start.2 = (bf16[16,2048]{1,0:T(8,128)(2,1)S(1)}, bf16[16,2048]{1,0:T(8,128)(2,1)S(1)}, u32[]{:S(2)}, u32[]{:S(2)}) collective-permute-start(bf16[16,2048]{1,0:T(8,128)(2,1)S(1)} %collective-permute-done.1), channel_id=1, source_target_pairs={{0,1},{1,2},{2,3},{3,4},{4,5},{5,6},{6,7},{7,0},{8,9},{9,10},{10,1... | collective-permute-start | bytes 196616 | tf_op jit(solution)/shard_map/ppermute | solution.py:61
  35.8 15.8 %collective-permute-start.3 = (bf16[16,2048]{1,0:T(8,128)(2,1)S(1)}, bf16[16,2048]{1,0:T(8,128)(2,1)S(1)}, u32[]{:S(2)}, u32[]{:S(2)}) collective-permute-start(bf16[16,2048]{1,0:T(8,128)(2,1)S(1)} %collective-permute-done.2), channel_id=1, source_target_pairs={{0,1},{1,2},{2,3},{3,4},{4,5},{5,6},{6,7},{7,0},{8,9},{9,10},{10,1... | collective-permute-start | bytes 196616 | tf_op jit(solution)/shard_map/ppermute | solution.py:61
  51.7 5.5 collective-permute-start.4
  57.2 5.5 collective-permute-start.5
  62.7 5.5 collective-permute-start.6
  81.1 119.7 %reduce-scatter.10.cloned.1.call-start = ((), (), s32[]{:S(2)}) async-start(), calls=%async_computation.8 | async-start | bytes 1179648 | tf_op jit(solution)/shard_map/reduce_scatter | solution.py:72
  113.1 5.6 collective-permute-start.7
  119.0 5.5 collective-permute-start.8
  124.5 5.5 collective-permute-start.9
  130.0 5.5 collective-permute-start.10
  135.5 5.5 collective-permute-start.11
  141.0 5.5 collective-permute-start.12
  146.5 5.5 collective-permute-start.13
  152.0 5.5 collective-permute-start.14
  169.4 120.2 %reduce-scatter.12.cloned.1.call-start = ((), (), s32[]{:S(2)}) async-start(), calls=%async_computation.9 | async-start | bytes 1179648 | tf_op jit(solution)/shard_map/reduce_scatter | solution.py:72
  201.7 5.6 collective-permute-start.15
  207.5 5.5 collective-permute-start.16
  213.0 5.5 collective-permute-start.17
  218.5 5.5 collective-permute-start.18
  224.0 5.5 collective-permute-start.19
  229.5 5.5 collective-permute-start.20
  235.0 5.5 collective-permute-start.21
  240.5 5.5 collective-permute-start.22
  258.0 119.9 %reduce-scatter.14.cloned.1.call-start = ((), (), s32[]{:S(2)}) async-start(), calls=%async_computation.10 | async-start | bytes 1179648 | tf_op jit(solution)/shard_map/reduce_scatter | solution.py:72
  296.2 5.5 collective-permute-start.24
  301.7 5.5 collective-permute-start.25
  307.2 5.5 collective-permute-start.26
  312.7 5.5 collective-permute-start.27
  318.2 5.5 collective-permute-start.28
  323.7 5.5 collective-permute-start.29
  329.2 5.5 collective-permute-start.30
  346.7 119.9 %reduce-scatter.16.cloned.1.call-start = ((), (), s32[]{:S(2)}) async-start(), calls=%async_computation.11 | async-start | bytes 1179648 | tf_op jit(solution)/shard_map/reduce_scatter | solution.py:72
  378.9 5.5 collective-permute-start.31
  384.6 5.5 collective-permute-start.32
  390.2 5.5 collective-permute-start.33
  395.7 5.5 collective-permute-start.34
  412.1 5.5 collective-permute-start.37
  435.1 120.2 %reduce-scatter.18.cloned.1.call-start = ((), (), s32[]{:S(2)}) async-start(), calls=%async_computation.12 | async-start | bytes 1179648 | tf_op jit(solution)/shard_map/reduce_scatter | solution.py:72
  473.3 5.8 collective-permute-start.40
  484.5 5.5 collective-permute-start.42
  501.0 5.5 collective-permute-start.45
  523.9 120.1 %reduce-scatter.20.cloned.1.call-start = ((), (), s32[]{:S(2)}) async-start(), calls=%async_computation.13 | async-start | bytes 1179648 | tf_op jit(solution)/shard_map/reduce_scatter | solution.py:72
  561.9 5.5 collective-permute-start.48
  578.4 5.5 collective-permute-start.51
  583.9 5.5 collective-permute-start.52
  (16 other events, 161.4 us)
Sparse Core Ops, SparseCore 0:
  81.2 30.9 reduce-scatter.7
  169.5 31.1 reduce-scatter.9
  258.1 31.4 reduce-scatter.11
  346.8 31.0 reduce-scatter.13
  435.3 31.3 reduce-scatter.15
  524.0 31.2 reduce-scatter.17
  612.4 31.5 reduce-scatter.19
